TPU v7x, 512 devices: a whole 4x8x8 slice. The times are simulated.
512 devices in a mesh: grid: 64 (over x, z, core), orb: 8 (over y).
Axes of the slice: x: 4, y: 8, z: 8, core: 2. Of those that a mesh axis runs over, the one named last changes fastest.
Arguments:
- orbitals: float32 [256, 16, 16, 1024], P('grid', None, None, 'orb'), may hold values from -15 to 15
- potential: float32 [256, 16, 16], P('grid'), may hold values from -2 to 0
Outputs:
- filtered: float32 [256, 16, 16, 1024], P('grid', None, None, 'orb')
- hamiltonian_block: float32 [1024, 1024], P('orb', 'grid')
- margin_block: float32 [1024, 1024], P('orb', 'grid')
All inputs are finite; a program needn't handle non-finite values.
Results may differ from a plain program's by a relative error of at most 0.0039.
Values may be sent and summed in bfloat16 or wider, within the bound.
No kernel may reach another device: no remote copies, remote signals or barrier semaphores. Data moves between devices by JAX's collectives and lax.ppermute only.
A program may use at most 64 MiB of HBM per device.

v0:
```python
import jax
import jax.numpy as jnp
from jax import lax
from jax.sharding import PartitionSpec as P

DEGREE = 4
STENCIL = (-205.0 / 72.0, 8.0 / 5.0, -1.0 / 5.0, 8.0 / 315.0, -1.0 / 560.0)
LOWER_EDGE = -2.0
CUT_EDGE = 1.5
UPPER_EDGE = 10.0
EPSILON = 1e-06


def halo_layers(shard, width):
    size = lax.axis_size("grid")
    length = shard.shape[0]
    up = [(i, i + 1) for i in range(size - 1)]
    down = [(j, i) for i, j in up]
    last = lax.slice_in_dim(shard, length - width, length, axis=0).astype(jnp.bfloat16)
    initial = lax.slice_in_dim(shard, 0, width, axis=0).astype(jnp.bfloat16)
    before = lax.ppermute(last, "grid", up).astype(shard.dtype)
    after = lax.ppermute(initial, "grid", down).astype(shard.dtype)
    return jnp.concatenate([before, shard, after], axis=0)


def plane_matrix(rows_y, cols_x):
    flat_count = rows_y * cols_x
    index_all = jnp.arange(flat_count, dtype=jnp.int32)
    row_y = (index_all // cols_x)[:, None]
    row_x = (index_all % cols_x)[:, None]
    col_y = (index_all // cols_x)[None, :]
    col_x = (index_all % cols_x)[None, :]
    delta_y = jnp.mod(row_y - col_y, rows_y)
    delta_x = jnp.mod(row_x - col_x, cols_x)
    same_y = delta_y == 0
    same_x = delta_x == 0
    matrix = jnp.zeros((flat_count, flat_count), jnp.float32)
    for offset in range(1, 5):
        for signed in (offset, -offset):
            hit_y = jnp.logical_and(same_x, delta_y == signed % rows_y)
            hit_x = jnp.logical_and(same_y, delta_x == signed % cols_x)
            matrix = matrix + STENCIL[offset] * (
                hit_y.astype(jnp.float32) + hit_x.astype(jnp.float32)
            )
    return matrix


def apply_hamiltonian(current, potential, plane):
    layers, rows_y, cols_x, width = current.shape
    padded = halo_layers(current, 4)
    laplacian = 3.0 * STENCIL[0] * current
    for offset in range(1, 5):
        laplacian = laplacian + STENCIL[offset] * (
            padded[4 + offset : 4 + offset + layers] + padded[4 - offset : 4 - offset + layers]
        )
    flat = current.reshape(layers, rows_y * cols_x, width)
    in_plane = jnp.einsum(
        "pq,zqo->zpo",
        plane,
        flat,
        precision=lax.Precision.HIGHEST,
        preferred_element_type=jnp.float32,
    )
    laplacian = laplacian + in_plane.reshape(current.shape)
    return -0.5 * laplacian + potential[:, :, :, None] * current


def chebyshev(initial, potential, plane):
    half_width = (UPPER_EDGE - CUT_EDGE) / 2.0
    centre = (UPPER_EDGE + CUT_EDGE) / 2.0
    sigma_now = half_width / (LOWER_EDGE - centre)
    gamma_ratio = 2.0 / sigma_now
    previous = initial
    current = (
        sigma_now / half_width * (apply_hamiltonian(previous, potential, plane) - centre * previous)
    )
    for degree_step in range(DEGREE - 1):
        sigma_next = 1.0 / (gamma_ratio - sigma_now)
        following = (
            2.0
            * sigma_next
            / half_width
            * (apply_hamiltonian(current, potential, plane) - centre * current)
            - sigma_now * sigma_next * previous
        )
        previous, current, sigma_now = (current, following, sigma_next)
    return current


def contract_points(left_side, right_side):
    return lax.dot_general(
        left_side, right_side, (((0,), (0,)), ((), ())), preferred_element_type=jnp.float32
    )


def reduce_scatter_grid(slots):
    size = slots.shape[0]
    bits = size.bit_length() - 1
    me = lax.axis_index("grid")
    rest = slots.shape[1:]
    buf = slots.reshape((2,) * bits + rest)
    for bit in range(bits):
        axis = bits - 1 - bit
        mine = me >> bit & 1
        low = lax.index_in_dim(buf, 0, axis=axis, keepdims=False)
        high = lax.index_in_dim(buf, 1, axis=axis, keepdims=False)
        keep = jnp.where(mine == 1, high, low)
        send = jnp.where(mine == 1, low, high)
        pairs = [(i, i ^ 1 << bit) for i in range(size)]
        buf = keep + lax.ppermute(send, "grid", pairs)
    return buf


def on_device(orbitals, potential):
    own_width = orbitals.shape[3]
    point_count = orbitals.shape[0] * orbitals.shape[1] * orbitals.shape[2]
    grid_size = lax.axis_size("grid")
    point_total = float(point_count * grid_size)
    plane = plane_matrix(orbitals.shape[1], orbitals.shape[2])
    result_block = chebyshev(orbitals, potential, plane)
    own_squares = jnp.sum(result_block * result_block, axis=(0, 1, 2))
    rounded_orbitals = result_block.astype(jnp.bfloat16).reshape(point_count, own_width)
    rounded_image = (
        apply_hamiltonian(result_block, potential, plane)
        .astype(jnp.bfloat16)
        .reshape(point_count, own_width)
    )
    orbitals_all = lax.all_gather(rounded_orbitals, "orb", axis=1, tiled=True)
    total_width = orbitals_all.shape[1]
    rows = total_width // grid_size
    hamiltonian_part = contract_points(orbitals_all, rounded_image)
    margin_part = contract_points(orbitals_all, rounded_orbitals)
    wide = orbitals_all.astype(jnp.float32)
    column_squares = jnp.sum(wide * wide, axis=0)
    body = jnp.concatenate(
        [
            hamiltonian_part.reshape(grid_size, rows, own_width),
            margin_part.reshape(grid_size, rows, own_width),
        ],
        axis=2,
    )
    tail = jnp.concatenate(
        [
            column_squares.reshape(grid_size, rows),
            jnp.broadcast_to(own_squares[None, :], (grid_size, own_width)),
            jnp.zeros((grid_size, own_width - rows), jnp.float32),
        ],
        axis=1,
    )
    slots = jnp.concatenate([body, tail[:, None, :]], axis=1)
    combined = reduce_scatter_grid(slots)
    scale_own = 1.0 / jnp.sqrt(combined[rows, rows : rows + own_width] / point_total + EPSILON)
    column_scale = 1.0 / jnp.sqrt(combined[rows, :rows] / point_total + EPSILON)
    filtered = result_block * scale_own
    pair_scale = scale_own[:, None] * column_scale[None, :] / point_total
    hamiltonian_block = combined[:rows, :own_width].T * pair_scale
    margin_block = combined[:rows, own_width:].T * pair_scale
    return (filtered, hamiltonian_block, margin_block)


def solution(mesh):
    placed = (P("grid", None, None, "orb"), P("grid", None, None))
    return jax.shard_map(
        on_device,
        mesh=mesh,
        in_specs=placed,
        out_specs=(P("grid", None, None, "orb"), P("orb", "grid"), P("orb", "grid")),
        check_vma=False,
    )
```

profile of v0, /device:TPU:2, one launch (start us, length us, event | category | flops | bytes accessed | tf_op | source)
XLA Modules:
  0.0 181.1 jit_solution(14058231074587495252)
XLA Ops:
  8.3 10.4 %collective-permute-start = (bf16[4,16,16,128]{3,2,1,0:T(8,128)(2,1)S(1)}, bf16[4,16,16,128]{3,2,1,0:T(8,128)(2,1)S(1)}, u32[]{:S(2)}, u32[]{:S(2)}) collective-permute-start(bf16[4,16,16,128]{3,2,1,0:T(8,128)(2,1)S(1)} %convert_element_type.233), channel_id=1, source_target_pairs={{8,0},{16,8},{24,16},{32,24},{40,32},{48,40},{56,48},{64,56},{72,6... | collective-permute-start | bytes 786440 | tf_op jit(solution)/shard_map/ppermute | solution.py:22
  21.4 2.7 %fusion.102 = f32[256,4,128]{2,0,1:T(8,128)S(1)} fusion(f32[4,256,128]{2,1,0:T(8,128)} %bitcast.96, s32[256]{0:T(256)S(1)} %get-tuple-element.22, s32[256]{0:T(256)S(1)} %get-tuple-element.23), kind=kOutput, calls=%fused_computation.176 | convolution fusion | flops 408944640 | bytes 1050624 | tf_op jit(solution)/shard_map/pq,zqo->zpo/dot_general | solution.py:57
  24.2 4.3 %collective-permute-done.1 = bf16[4,16,16,128]{3,2,1,0:T(8,128)(2,1)S(1)} collective-permute-done((bf16[4,16,16,128]{3,2,1,0:T(8,128)(2,1)S(1)}, bf16[4,16,16,128]{3,2,1,0:T(8,128)(2,1)S(1)}, u32[]{:S(2)}, u32[]{:S(2)}) %collective-permute-start.1) | collective-permute-done | bytes 262176 | tf_op jit(solution)/shard_map/ppermute | solution.py:21
  30.8 2.4 %collective-permute-start.3 = (bf16[4,16,16,128]{3,2,1,0:T(8,128)(2,1)S(1)}, bf16[4,16,16,128]{3,2,1,0:T(8,128)(2,1)S(1)}, u32[]{:S(2)}, u32[]{:S(2)}) collective-permute-start(bf16[4,16,16,128]{3,2,1,0:T(8,128)(2,1)S(1)} %get-tuple-element.9), channel_id=1, source_target_pairs={{0,8},{8,16},{16,24},{24,32},{32,40},{40,48},{48,56},{56,64},{64,7... | collective-permute-start | bytes 786440 | tf_op jit(solution)/shard_map/ppermute | solution.py:21
  35.5 5.1 %collective-permute-done.3 = bf16[4,16,16,128]{3,2,1,0:T(8,128)(2,1)S(1)} collective-permute-done((bf16[4,16,16,128]{3,2,1,0:T(8,128)(2,1)S(1)}, bf16[4,16,16,128]{3,2,1,0:T(8,128)(2,1)S(1)}, u32[]{:S(2)}, u32[]{:S(2)}) %collective-permute-start.3) | collective-permute-done | bytes 262176 | tf_op jit(solution)/shard_map/ppermute | solution.py:21
  43.1 2.4 %collective-permute-start.5 = (bf16[4,16,16,128]{3,2,1,0:T(8,128)(2,1)S(1)}, bf16[4,16,16,128]{3,2,1,0:T(8,128)(2,1)S(1)}, u32[]{:S(2)}, u32[]{:S(2)}) collective-permute-start(bf16[4,16,16,128]{3,2,1,0:T(8,128)(2,1)S(1)} %get-tuple-element.7), channel_id=1, source_target_pairs={{0,8},{8,16},{16,24},{24,32},{32,40},{40,48},{48,56},{56,64},{64,7... | collective-permute-start | bytes 786440 | tf_op jit(solution)/shard_map/ppermute | solution.py:21
  45.5 1.9 %convolution_bitcast_fusion.2 = f32[4,256,128]{1,2,0:T(8,128)S(1)} fusion(f32[4,256,128]{2,1,0:T(8,128)S(1)} %bitcast.97, s32[256]{0:T(256)S(1)} %get-tuple-element.22, s32[256]{0:T(256)S(1)} %get-tuple-element.23), kind=kOutput, calls=%fused_computation.43 | convolution fusion | flops 408944640 | bytes 1050624 | tf_op jit(solution)/shard_map/pq,zqo->zpo/dot_general | solution.py:57
  47.7 5.2 %collective-permute-done.5 = bf16[4,16,16,128]{3,2,1,0:T(8,128)(2,1)S(1)} collective-permute-done((bf16[4,16,16,128]{3,2,1,0:T(8,128)(2,1)S(1)}, bf16[4,16,16,128]{3,2,1,0:T(8,128)(2,1)S(1)}, u32[]{:S(2)}, u32[]{:S(2)}) %collective-permute-start.5) | collective-permute-done | bytes 262176 | tf_op jit(solution)/shard_map/ppermute | solution.py:21
  55.2 2.4 %collective-permute-start.7 = (bf16[4,16,16,128]{3,2,1,0:T(8,128)(2,1)S(1)}, bf16[4,16,16,128]{3,2,1,0:T(8,128)(2,1)S(1)}, u32[]{:S(2)}, u32[]{:S(2)}) collective-permute-start(bf16[4,16,16,128]{3,2,1,0:T(8,128)(2,1)S(1)} %get-tuple-element.5), channel_id=1, source_target_pairs={{0,8},{8,16},{16,24},{24,32},{32,40},{40,48},{48,56},{56,64},{64,7... | collective-permute-start | bytes 786440 | tf_op jit(solution)/shard_map/ppermute | solution.py:21
  59.8 5.2 %collective-permute-done.7 = bf16[4,16,16,128]{3,2,1,0:T(8,128)(2,1)S(1)} collective-permute-done((bf16[4,16,16,128]{3,2,1,0:T(8,128)(2,1)S(1)}, bf16[4,16,16,128]{3,2,1,0:T(8,128)(2,1)S(1)}, u32[]{:S(2)}, u32[]{:S(2)}) %collective-permute-start.7) | collective-permute-done | bytes 262176 | tf_op jit(solution)/shard_map/ppermute | solution.py:21
  68.3 5.9 %collective-permute-start.8 = (bf16[4,16,16,128]{3,2,1,0:T(8,128)(2,1)}, bf16[4,16,16,128]{3,2,1,0:T(8,128)(2,1)S(1)}, u32[]{:S(2)}, u32[]{:S(2)}) collective-permute-start(bf16[4,16,16,128]{3,2,1,0:T(8,128)(2,1)} %convert_element_type.261), channel_id=1, source_target_pairs={{8,0},{16,8},{24,16},{32,24},{40,32},{48,40},{56,48},{64,56},{72,6... | collective-permute-start | bytes 786440 | tf_op jit(solution)/shard_map/ppermute | solution.py:22
  78.6 34.1 %all-gather.2.cloned.1.call-done = bf16[1024,1024]{1,0:T(8,128)(2,1)} async-done(((bf16[1024,128]{1,0:T(8,128)(2,1)}), bf16[1024,1024]{1,0:T(8,128)(2,1)}) %all-gather.2.cloned.1.call-update) | async-done | bytes 2097168 | tf_op jit(solution)/shard_map/all_gather | solution.py:128
  112.8 2.1 %multiply_reduce_fusion = f32[1024]{0:T(1024)S(1)} fusion(bf16[1024,1024]{1,0:T(8,128)(2,1)} %all-gather.2.cloned.1.call-done), kind=kLoop, calls=%fused_computation | loop fusion | flops 3144704 | bytes 2101248 | tf_op jit(solution)/shard_map/reduce_sum | solution.py:134
  115.0 2.9 %copy.191 = bf16[1024,1024]{1,0:T(8,128)(2,1)S(1)} copy(bf16[1024,1024]{0,1:T(8,128)(2,1)} %bitcast.94) | data formatting | bytes 4194304 | tf_op jit(solution)/shard_map/dot_general | solution.py:91
  124.3 2.1 %collective-permute-done.10 = f32[2,2,2,2,2,17,256]{6,4,5,3,2,1,0:T(2,128)S(1)} collective-permute-done((f32[2,2,2,2,2,17,256]{6,4,5,3,2,1,0:T(2,128)}, f32[2,2,2,2,2,17,256]{6,4,5,3,2,1,0:T(2,128)S(1)}, u32[]{:S(2)}, u32[]{:S(2)}) %collective-permute-start.10) | collective-permute-done | bytes 557088 | tf_op jit(solution)/shard_map/ppermute | solution.py:110
  127.0 3.6 %collective-permute-start.11 = (f32[2,2,2,2,17,256]{5,3,4,2,1,0:T(2,128)S(1)}, f32[2,2,2,2,17,256]{5,3,4,2,1,0:T(2,128)S(1)}, u32[]{:S(2)}, u32[]{:S(2)}) collective-permute-start(f32[2,2,2,2,17,256]{5,3,4,2,1,0:T(2,128)S(1)} %select_bitcast_fusion.1), channel_id=1, source_target_pairs={{0,16},{8,24},{16,0},{24,8},{32,48},{40,56},{48,32},{56,40},{64,80... | collective-permute-start | bytes 835592 | tf_op jit(solution)/shard_map/ppermute | solution.py:110
  130.6 7.0 %collective-permute-done.11 = f32[2,2,2,2,17,256]{5,3,4,2,1,0:T(2,128)S(1)} collective-permute-done((f32[2,2,2,2,17,256]{5,3,4,2,1,0:T(2,128)S(1)}, f32[2,2,2,2,17,256]{5,3,4,2,1,0:T(2,128)S(1)}, u32[]{:S(2)}, u32[]{:S(2)}) %collective-permute-start.11) | collective-permute-done | bytes 278560 | tf_op jit(solution)/shard_map/ppermute | solution.py:110
  138.1 4.6 %collective-permute-start.12 = (f32[2,2,2,17,256]{4,2,3,1,0:T(2,128)S(1)}, f32[2,2,2,17,256]{4,2,3,1,0:T(2,128)S(1)}, u32[]{:S(2)}, u32[]{:S(2)}) collective-permute-start(f32[2,2,2,17,256]{4,2,3,1,0:T(2,128)S(1)} %bitcast.109), channel_id=1, source_target_pairs={{0,32},{8,40},{16,48},{24,56},{32,0},{40,8},{48,16},{56,24},{64,96... | collective-permute-start | bytes 417800 | tf_op jit(solution)/shard_map/ppermute | solution.py:110
  142.8 6.1 %collective-permute-done.12 = f32[2,2,2,17,256]{4,2,3,1,0:T(2,128)S(1)} collective-permute-done((f32[2,2,2,17,256]{4,2,3,1,0:T(2,128)S(1)}, f32[2,2,2,17,256]{4,2,3,1,0:T(2,128)S(1)}, u32[]{:S(2)}, u32[]{:S(2)}) %collective-permute-start.12) | collective-permute-done | bytes 139296 | tf_op jit(solution)/shard_map/ppermute | solution.py:110
  149.1 7.9 %collective-permute-start.13 = (f32[2,2,17,256]{3,1,2,0:T(2,128)S(1)}, f32[2,2,17,256]{3,1,2,0:T(2,128)S(1)}, u32[]{:S(2)}, u32[]{:S(2)}) collective-permute-start(f32[2,2,17,256]{3,1,2,0:T(2,128)S(1)} %bitcast.110), channel_id=1, source_target_pairs={{0,64},{8,72},{16,80},{24,88},{32,96},{40,104},{48,112},{56,120},{... | collective-permute-start | bytes 208904 | tf_op jit(solution)/shard_map/ppermute | solution.py:110
  157.0 2.3 %collective-permute-done.13 = f32[2,2,17,256]{3,1,2,0:T(2,128)S(1)} collective-permute-done((f32[2,2,17,256]{3,1,2,0:T(2,128)S(1)}, f32[2,2,17,256]{3,1,2,0:T(2,128)S(1)}, u32[]{:S(2)}, u32[]{:S(2)}) %collective-permute-start.13) | collective-permute-done | bytes 69664 | tf_op jit(solution)/shard_map/ppermute | solution.py:110
  159.5 4.0 %collective-permute-start.14 = (f32[2,17,256]{2,0,1:T(2,128)S(1)}, f32[2,17,256]{2,0,1:T(2,128)S(1)}, u32[]{:S(2)}, u32[]{:S(2)}) collective-permute-start(f32[2,17,256]{2,0,1:T(2,128)S(1)} %bitcast.111), channel_id=1, source_target_pairs={{0,128},{8,136},{16,144},{24,152},{32,160},{40,168},{48,176},{56,1... | collective-permute-start | bytes 104456 | tf_op jit(solution)/shard_map/ppermute | solution.py:110
  165.5 3.9 %collective-permute-start.15 = (f32[17,256]{1,0:T(8,128)S(1)}, f32[17,256]{1,0:T(8,128)S(1)}, u32[]{:S(2)}, u32[]{:S(2)}) collective-permute-start(f32[17,256]{1,0:T(8,128)S(1)} %bitcast.112), channel_id=1, source_target_pairs={{0,256},{8,264},{16,272},{24,280},{32,288},{40,296},{48,304},{56,3... | collective-permute-start | bytes 52232 | tf_op jit(solution)/shard_map/ppermute | solution.py:110
  169.4 3.3 %collective-permute-done.15 = f32[17,256]{1,0:T(8,128)S(1)} collective-permute-done((f32[17,256]{1,0:T(8,128)S(1)}, f32[17,256]{1,0:T(8,128)S(1)}, u32[]{:S(2)}, u32[]{:S(2)}) %collective-permute-start.15) | collective-permute-done | bytes 17440 | tf_op jit(solution)/shard_map/ppermute | solution.py:110
  (79 shorter events, 34.6 us)
Async XLA Ops:
  7.2 105.6 %all-gather.2.cloned.1.call-start = ((), (), s32[]{:S(2)}) async-start(), calls=%async_computation | async-start | bytes 2359296 | tf_op jit(solution)/shard_map/all_gather | solution.py:128
  8.3 15.8 %collective-permute-start = (bf16[4,16,16,128]{3,2,1,0:T(8,128)(2,1)S(1)}, bf16[4,16,16,128]{3,2,1,0:T(8,128)(2,1)S(1)}, u32[]{:S(2)}, u32[]{:S(2)}) collective-permute-start(bf16[4,16,16,128]{3,2,1,0:T(8,128)(2,1)S(1)} %convert_element_type.233), channel_id=1, source_target_pairs={{8,0},{16,8},{24,16},{32,24},{40,32},{48,40},{56,48},{64,56},{72,6... | collective-permute-start | bytes 786440 | tf_op jit(solution)/shard_map/ppermute | solution.py:22
  18.7 9.8 %collective-permute-start.1 = (bf16[4,16,16,128]{3,2,1,0:T(8,128)(2,1)S(1)}, bf16[4,16,16,128]{3,2,1,0:T(8,128)(2,1)S(1)}, u32[]{:S(2)}, u32[]{:S(2)}) collective-permute-start(bf16[4,16,16,128]{3,2,1,0:T(8,128)(2,1)S(1)} %convert_element_type.233), channel_id=1, source_target_pairs={{0,8},{8,16},{16,24},{24,32},{32,40},{40,48},{48,56},{56,64},{64,7... | collective-permute-start | bytes 786440 | tf_op jit(solution)/shard_map/ppermute | solution.py:21
  21.4 7.1 %copy-start = (f32[4,16,16,128]{3,2,1,0:T(8,128)S(1)}, f32[4,16,16,128]{3,2,1,0:T(8,128)}, u32[]{:S(2)}) copy-start(f32[4,16,16,128]{3,2,1,0:T(8,128)} %param.2) | copy-start | bytes 1572868
  21.4 7.2 %copy-start.2 = (f32[4,16,16]{2,1,0:T(8,128)S(1)}, f32[4,16,16]{2,1,0:T(8,128)}, u32[]{:S(2)}) copy-start(f32[4,16,16]{2,1,0:T(8,128)} %param.3) | copy-start | bytes 12292
  28.9 6.5 %collective-permute-start.2 = (bf16[4,16,16,128]{3,2,1,0:T(8,128)(2,1)S(1)}, bf16[4,16,16,128]{3,2,1,0:T(8,128)(2,1)S(1)}, u32[]{:S(2)}, u32[]{:S(2)}) collective-permute-start(bf16[4,16,16,128]{3,2,1,0:T(8,128)(2,1)S(1)} %get-tuple-element.9), channel_id=1, source_target_pairs={{8,0},{16,8},{24,16},{32,24},{40,32},{48,40},{56,48},{64,56},{72,6... | collective-permute-start | bytes 786440 | tf_op jit(solution)/shard_map/ppermute | solution.py:22
  30.8 9.8 %collective-permute-start.3 = (bf16[4,16,16,128]{3,2,1,0:T(8,128)(2,1)S(1)}, bf16[4,16,16,128]{3,2,1,0:T(8,128)(2,1)S(1)}, u32[]{:S(2)}, u32[]{:S(2)}) collective-permute-start(bf16[4,16,16,128]{3,2,1,0:T(8,128)(2,1)S(1)} %get-tuple-element.9), channel_id=1, source_target_pairs={{0,8},{8,16},{16,24},{24,32},{32,40},{40,48},{48,56},{56,64},{64,7... | collective-permute-start | bytes 786440 | tf_op jit(solution)/shard_map/ppermute | solution.py:21
  41.1 6.5 %collective-permute-start.4 = (bf16[4,16,16,128]{3,2,1,0:T(8,128)(2,1)S(1)}, bf16[4,16,16,128]{3,2,1,0:T(8,128)(2,1)S(1)}, u32[]{:S(2)}, u32[]{:S(2)}) collective-permute-start(bf16[4,16,16,128]{3,2,1,0:T(8,128)(2,1)S(1)} %get-tuple-element.7), channel_id=1, source_target_pairs={{8,0},{16,8},{24,16},{32,24},{40,32},{48,40},{56,48},{64,56},{72,6... | collective-permute-start | bytes 786440 | tf_op jit(solution)/shard_map/ppermute | solution.py:22
  43.1 9.8 %collective-permute-start.5 = (bf16[4,16,16,128]{3,2,1,0:T(8,128)(2,1)S(1)}, bf16[4,16,16,128]{3,2,1,0:T(8,128)(2,1)S(1)}, u32[]{:S(2)}, u32[]{:S(2)}) collective-permute-start(bf16[4,16,16,128]{3,2,1,0:T(8,128)(2,1)S(1)} %get-tuple-element.7), channel_id=1, source_target_pairs={{0,8},{8,16},{16,24},{24,32},{32,40},{40,48},{48,56},{56,64},{64,7... | collective-permute-start | bytes 786440 | tf_op jit(solution)/shard_map/ppermute | solution.py:21
  53.3 6.5 %collective-permute-start.6 = (bf16[4,16,16,128]{3,2,1,0:T(8,128)(2,1)S(1)}, bf16[4,16,16,128]{3,2,1,0:T(8,128)(2,1)S(1)}, u32[]{:S(2)}, u32[]{:S(2)}) collective-permute-start(bf16[4,16,16,128]{3,2,1,0:T(8,128)(2,1)S(1)} %get-tuple-element.5), channel_id=1, source_target_pairs={{8,0},{16,8},{24,16},{32,24},{40,32},{48,40},{56,48},{64,56},{72,6... | collective-permute-start | bytes 786440 | tf_op jit(solution)/shard_map/ppermute | solution.py:22
  55.2 9.8 %collective-permute-start.7 = (bf16[4,16,16,128]{3,2,1,0:T(8,128)(2,1)S(1)}, bf16[4,16,16,128]{3,2,1,0:T(8,128)(2,1)S(1)}, u32[]{:S(2)}, u32[]{:S(2)}) collective-permute-start(bf16[4,16,16,128]{3,2,1,0:T(8,128)(2,1)S(1)} %get-tuple-element.5), channel_id=1, source_target_pairs={{0,8},{8,16},{16,24},{24,32},{32,40},{40,48},{48,56},{56,64},{64,7... | collective-permute-start | bytes 786440 | tf_op jit(solution)/shard_map/ppermute | solution.py:21
  66.4 10.1 %collective-permute-start.9 = (bf16[4,16,16,128]{3,2,1,0:T(8,128)(2,1)}, bf16[4,16,16,128]{3,2,1,0:T(8,128)(2,1)S(1)}, u32[]{:S(2)}, u32[]{:S(2)}) collective-permute-start(bf16[4,16,16,128]{3,2,1,0:T(8,128)(2,1)} %convert_element_type.261), channel_id=1, source_target_pairs={{0,8},{8,16},{16,24},{24,32},{32,40},{40,48},{48,56},{56,64},{64,7... | collective-permute-start | bytes 786440 | tf_op jit(solution)/shard_map/ppermute | solution.py:21
  68.3 9.9 %collective-permute-start.8 = (bf16[4,16,16,128]{3,2,1,0:T(8,128)(2,1)}, bf16[4,16,16,128]{3,2,1,0:T(8,128)(2,1)S(1)}, u32[]{:S(2)}, u32[]{:S(2)}) collective-permute-start(bf16[4,16,16,128]{3,2,1,0:T(8,128)(2,1)} %convert_element_type.261), channel_id=1, source_target_pairs={{8,0},{16,8},{24,16},{32,24},{40,32},{48,40},{56,48},{64,56},{72,6... | collective-permute-start | bytes 786440 | tf_op jit(solution)/shard_map/ppermute | solution.py:22
  115.0 2.9 %copy-start.1 = (bf16[4,16,16,128]{3,2,1,0:T(8,128)(2,1)S(1)}, bf16[4,16,16,128]{3,2,1,0:T(8,128)(2,1)}, u32[]{:S(2)}) copy-start(bf16[4,16,16,128]{3,2,1,0:T(8,128)(2,1)} %convert_element_type.261) | copy-start | bytes 786436
  122.4 4.0 %collective-permute-start.10 = (f32[2,2,2,2,2,17,256]{6,4,5,3,2,1,0:T(2,128)}, f32[2,2,2,2,2,17,256]{6,4,5,3,2,1,0:T(2,128)S(1)}, u32[]{:S(2)}, u32[]{:S(2)}) collective-permute-start(f32[2,2,2,2,2,17,256]{6,4,5,3,2,1,0:T(2,128)} %copy.196), channel_id=1, source_target_pairs={{0,8},{8,0},{16,24},{24,16},{32,40},{40,32},{48,56},{56,48},{64,72... | collective-permute-start | bytes 1671176 | tf_op jit(solution)/shard_map/ppermute | solution.py:110
  127.0 10.6 %collective-permute-start.11 = (f32[2,2,2,2,17,256]{5,3,4,2,1,0:T(2,128)S(1)}, f32[2,2,2,2,17,256]{5,3,4,2,1,0:T(2,128)S(1)}, u32[]{:S(2)}, u32[]{:S(2)}) collective-permute-start(f32[2,2,2,2,17,256]{5,3,4,2,1,0:T(2,128)S(1)} %select_bitcast_fusion.1), channel_id=1, source_target_pairs={{0,16},{8,24},{16,0},{24,8},{32,48},{40,56},{48,32},{56,40},{64,80... | collective-permute-start | bytes 835592 | tf_op jit(solution)/shard_map/ppermute | solution.py:110
  138.1 10.7 %collective-permute-start.12 = (f32[2,2,2,17,256]{4,2,3,1,0:T(2,128)S(1)}, f32[2,2,2,17,256]{4,2,3,1,0:T(2,128)S(1)}, u32[]{:S(2)}, u32[]{:S(2)}) collective-permute-start(f32[2,2,2,17,256]{4,2,3,1,0:T(2,128)S(1)} %bitcast.109), channel_id=1, source_target_pairs={{0,32},{8,40},{16,48},{24,56},{32,0},{40,8},{48,16},{56,24},{64,96... | collective-permute-start | bytes 417800 | tf_op jit(solution)/shard_map/ppermute | solution.py:110
  149.1 10.2 %collective-permute-start.13 = (f32[2,2,17,256]{3,1,2,0:T(2,128)S(1)}, f32[2,2,17,256]{3,1,2,0:T(2,128)S(1)}, u32[]{:S(2)}, u32[]{:S(2)}) collective-permute-start(f32[2,2,17,256]{3,1,2,0:T(2,128)S(1)} %bitcast.110), channel_id=1, source_target_pairs={{0,64},{8,72},{16,80},{24,88},{32,96},{40,104},{48,112},{56,120},{... | collective-permute-start | bytes 208904 | tf_op jit(solution)/shard_map/ppermute | solution.py:110
  159.5 5.9 %collective-permute-start.14 = (f32[2,17,256]{2,0,1:T(2,128)S(1)}, f32[2,17,256]{2,0,1:T(2,128)S(1)}, u32[]{:S(2)}, u32[]{:S(2)}) collective-permute-start(f32[2,17,256]{2,0,1:T(2,128)S(1)} %bitcast.111), channel_id=1, source_target_pairs={{0,128},{8,136},{16,144},{24,152},{32,160},{40,168},{48,176},{56,1... | collective-permute-start | bytes 104456 | tf_op jit(solution)/shard_map/ppermute | solution.py:110
  165.5 7.2 %collective-permute-start.15 = (f32[17,256]{1,0:T(8,128)S(1)}, f32[17,256]{1,0:T(8,128)S(1)}, u32[]{:S(2)}, u32[]{:S(2)}) collective-permute-start(f32[17,256]{1,0:T(8,128)S(1)} %bitcast.112), channel_id=1, source_target_pairs={{0,256},{8,264},{16,272},{24,280},{32,288},{40,296},{48,304},{56,3... | collective-permute-start | bytes 52232 | tf_op jit(solution)/shard_map/ppermute | solution.py:110
Sparse Core Ops, SparseCore 0:
  66.4 46.3 all-gather.1
where the time goes:
time: 182 us; the launch traced here: 181 us
  waiting for transfers between devices  78.5 us (43%)
  starting transfers between devices  59.1 us (32%)
  between operations  14.6 us (8%)
  matrix products  11.8 us (6%)
  other arithmetic  11 us (6%)
  local copies, waits for them, and re-layouts  6.16 us (3%)
    all_gather x1, waiting for transfers between devices, on_device(): orbitals_all = lax.all_gather(rounded_orbitals, 'orb', axis=1, tiled=True)  34.1 us
    ppermute x6, starting transfers between devices, reduce_scatter_grid(): buf = keep + lax.ppermute(send, 'grid', pairs)  25.9 us
    ppermute x6, waiting for transfers between devices, reduce_scatter_grid(): buf = keep + lax.ppermute(send, 'grid', pairs)  22.7 us
    ppermute x5, starting transfers between devices, halo_layers(): after = lax.ppermute(initial, 'grid', down).astype(shard.dtype)  22.1 us
    ppermute x5, waiting for transfers between devices, halo_layers(): before = lax.ppermute(last, 'grid', up).astype(shard.dtype)  19.8 us
    ppermute x5, starting transfers between devices, halo_layers(): before = lax.ppermute(last, 'grid', up).astype(shard.dtype)  11 us
    dot_general x5, matrix products, apply_hamiltonian(): jnp.einsum('pq,zqo->zpo', plane, flat, precision=lax.Precision.HIGHEST, p...  10.4 us
  transfers between devices with their start and end apart: 17, of which 12 were waited for; matrix products, arithmetic and copies ran while one was open for 7% of the time, Pallas kernels for 0%

commit v1 on v0

--- a/solution.py
+++ b/solution.py
@@ -9,6 +9,12 @@
 CUT_EDGE = 1.5
 UPPER_EDGE = 10.0
 EPSILON = 1e-06
+
+
+def joined_along(pieces, dim):
+    dims = list(pieces.shape[1:])
+    dims[dim] *= pieces.shape[0]
+    return jnp.moveaxis(pieces, 0, dim).reshape(dims)
 
 
 def halo_layers(shard, width):
@@ -125,7 +131,19 @@
         .astype(jnp.bfloat16)
         .reshape(point_count, own_width)
     )
-    orbitals_all = lax.all_gather(rounded_orbitals, "orb", axis=1, tiled=True)
+    peers = lax.axis_size("orb")
+    pairs_2 = [(i_2, (i_2 + 1) % peers) for i_2 in range(peers)]
+    back = [(b, a) for a, b in pairs_2]
+    lower, upper = ([], [])
+    for lap in range(peers - 1):
+        if lap % 2 == 0:
+            lower.append(lax.ppermute(lower[-1] if lower else rounded_orbitals, "orb", pairs_2))
+        else:
+            upper.append(lax.ppermute(upper[-1] if upper else rounded_orbitals, "orb", back))
+    blocks = jnp.stack([*lower[::-1], rounded_orbitals, *upper])
+    shift = lax.axis_index("orb") - len(lower)
+    blocks = blocks[(jnp.arange(peers) - shift) % peers]
+    orbitals_all = joined_along(blocks, 1)
     total_width = orbitals_all.shape[1]
     rows = total_width // grid_size
     hamiltonian_part = contract_points(orbitals_all, rounded_image)

time: 182 us -> 175 us (0.962)
  the two profiles are of different devices: /device:TPU:2 before, /device:TPU:30 now
where the time goes in v1:
time: 175 us; the launch traced here: 174 us
  starting transfers between devices  72.8 us (42%)
  waiting for transfers between devices  62.5 us (36%)
  local copies, waits for them, and re-layouts  15.2 us (9%)
  matrix products  13.6 us (8%)
  other arithmetic  8.68 us (5%)
    ppermute x6, waiting for transfers between devices, reduce_scatter_grid(): buf = keep + lax.ppermute(send, 'grid', pairs)  35.3 us
    ppermute x5, starting transfers between devices, halo_layers(): after = lax.ppermute(initial, 'grid', down).astype(shard.dtype)  22.2 us
    ppermute x4, starting transfers between devices, on_device(): lax.ppermute(lower[-1] if lower else rounded_orbitals, 'orb', pairs_2)  20.7 us
    ppermute x5, waiting for transfers between devices, halo_layers(): before = lax.ppermute(last, 'grid', up).astype(shard.dtype)  19.8 us
    ppermute x6, starting transfers between devices, reduce_scatter_grid(): buf = keep + lax.ppermute(send, 'grid', pairs)  13.1 us
    ppermute x5, starting transfers between devices, halo_layers(): before = lax.ppermute(last, 'grid', up).astype(shard.dtype)  11.1 us
    dot_general x5, matrix products, apply_hamiltonian(): jnp.einsum('pq,zqo->zpo', plane, flat, precision=lax.Precision.HIGHEST, p...  10.4 us
    unnamed x14, local copies, waits for them, and re-layouts  6.1 us
  transfers between devices with their start and end apart: 23, of which 13 were waited for; matrix products, arithmetic and copies ran while one was open for 11% of the time, Pallas kernels for 0%

profile of v1, /device:TPU:30, one launch (start us, length us, event | category | flops | bytes accessed | tf_op | source)
XLA Modules:
  0.0 174.0 jit_solution(16991870718522626047)
XLA Ops:
  1.7 10.7 %collective-permute-start = (bf16[4,16,16,128]{3,2,1,0:T(8,128)(2,1)S(1)}, bf16[4,16,16,128]{3,2,1,0:T(8,128)(2,1)S(1)}, u32[]{:S(2)}, u32[]{:S(2)}) collective-permute-start(bf16[4,16,16,128]{3,2,1,0:T(8,128)(2,1)S(1)} %convert_element_type.234), channel_id=1, source_target_pairs={{8,0},{16,8},{24,16},{32,24},{40,32},{48,40},{56,48},{64,56},{72,6... | collective-permute-start | bytes 786440 | tf_op jit(solution)/shard_map/ppermute | solution.py:28
  15.1 2.7 %fusion.102 = f32[256,4,128]{2,0,1:T(8,128)S(1)} fusion(f32[4,256,128]{2,1,0:T(8,128)} %bitcast.118, s32[256]{0:T(256)S(1)} %get-tuple-element.22, s32[256]{0:T(256)S(1)} %get-tuple-element.23), kind=kOutput, calls=%fused_computation.184 | convolution fusion | flops 408944640 | bytes 1050624 | tf_op jit(solution)/shard_map/pq,zqo->zpo/dot_general | solution.py:63
  17.9 4.3 %collective-permute-done.1 = bf16[4,16,16,128]{3,2,1,0:T(8,128)(2,1)S(1)} collective-permute-done((bf16[4,16,16,128]{3,2,1,0:T(8,128)(2,1)S(1)}, bf16[4,16,16,128]{3,2,1,0:T(8,128)(2,1)S(1)}, u32[]{:S(2)}, u32[]{:S(2)}) %collective-permute-start.1) | collective-permute-done | bytes 262176 | tf_op jit(solution)/shard_map/ppermute | solution.py:27
  24.6 2.4 %collective-permute-start.3 = (bf16[4,16,16,128]{3,2,1,0:T(8,128)(2,1)S(1)}, bf16[4,16,16,128]{3,2,1,0:T(8,128)(2,1)S(1)}, u32[]{:S(2)}, u32[]{:S(2)}) collective-permute-start(bf16[4,16,16,128]{3,2,1,0:T(8,128)(2,1)S(1)} %get-tuple-element.9), channel_id=1, source_target_pairs={{0,8},{8,16},{16,24},{24,32},{32,40},{40,48},{48,56},{56,64},{64,7... | collective-permute-start | bytes 786440 | tf_op jit(solution)/shard_map/ppermute | solution.py:27
  29.2 5.1 %collective-permute-done.3 = bf16[4,16,16,128]{3,2,1,0:T(8,128)(2,1)S(1)} collective-permute-done((bf16[4,16,16,128]{3,2,1,0:T(8,128)(2,1)S(1)}, bf16[4,16,16,128]{3,2,1,0:T(8,128)(2,1)S(1)}, u32[]{:S(2)}, u32[]{:S(2)}) %collective-permute-start.3) | collective-permute-done | bytes 262176 | tf_op jit(solution)/shard_map/ppermute | solution.py:27
  36.8 2.4 %collective-permute-start.5 = (bf16[4,16,16,128]{3,2,1,0:T(8,128)(2,1)S(1)}, bf16[4,16,16,128]{3,2,1,0:T(8,128)(2,1)S(1)}, u32[]{:S(2)}, u32[]{:S(2)}) collective-permute-start(bf16[4,16,16,128]{3,2,1,0:T(8,128)(2,1)S(1)} %get-tuple-element.7), channel_id=1, source_target_pairs={{0,8},{8,16},{16,24},{24,32},{32,40},{40,48},{48,56},{56,64},{64,7... | collective-permute-start | bytes 786440 | tf_op jit(solution)/shard_map/ppermute | solution.py:27
  41.4 5.2 %collective-permute-done.5 = bf16[4,16,16,128]{3,2,1,0:T(8,128)(2,1)S(1)} collective-permute-done((bf16[4,16,16,128]{3,2,1,0:T(8,128)(2,1)S(1)}, bf16[4,16,16,128]{3,2,1,0:T(8,128)(2,1)S(1)}, u32[]{:S(2)}, u32[]{:S(2)}) %collective-permute-start.5) | collective-permute-done | bytes 262176 | tf_op jit(solution)/shard_map/ppermute | solution.py:27
  53.6 5.2 %collective-permute-done.7 = bf16[4,16,16,128]{3,2,1,0:T(8,128)(2,1)S(1)} collective-permute-done((bf16[4,16,16,128]{3,2,1,0:T(8,128)(2,1)S(1)}, bf16[4,16,16,128]{3,2,1,0:T(8,128)(2,1)S(1)}, u32[]{:S(2)}, u32[]{:S(2)}) %collective-permute-start.7) | collective-permute-done | bytes 262176 | tf_op jit(solution)/shard_map/ppermute | solution.py:27
  59.3 4.7 %collective-permute-start.8 = (bf16[1024,128]{1,0:T(8,128)(2,1)S(1)}, bf16[1024,128]{1,0:T(8,128)(2,1)S(1)}, u32[]{:S(2)}, u32[]{:S(2)}) collective-permute-start(bf16[1024,128]{1,0:T(8,128)(2,1)S(1)} %bitcast.121), channel_id=1, source_target_pairs={{0,1},{1,2},{2,3},{3,4},{4,5},{5,6},{6,7},{7,0},{8,9},{9,10},{10,1... | collective-permute-start | bytes 786440 | tf_op jit(solution)/shard_map/ppermute | solution.py:140
  64.0 3.9 %collective-permute-done.8 = bf16[1024,128]{1,0:T(8,128)(2,1)S(1)} collective-permute-done((bf16[1024,128]{1,0:T(8,128)(2,1)S(1)}, bf16[1024,128]{1,0:T(8,128)(2,1)S(1)}, u32[]{:S(2)}, u32[]{:S(2)}) %collective-permute-start.8) | collective-permute-done | bytes 262176 | tf_op jit(solution)/shard_map/ppermute | solution.py:140
  67.9 5.6 %collective-permute-start.9 = (bf16[1024,128]{1,0:T(8,128)(2,1)S(1)}, bf16[1024,128]{1,0:T(8,128)(2,1)S(1)}, u32[]{:S(2)}, u32[]{:S(2)}) collective-permute-start(bf16[1024,128]{1,0:T(8,128)(2,1)S(1)} %collective-permute-done.8), channel_id=1, source_target_pairs={{0,1},{1,2},{2,3},{3,4},{4,5},{5,6},{6,7},{7,0},{8,9},{9,10},{10,1... | collective-permute-start | bytes 786440 | tf_op jit(solution)/shard_map/ppermute | solution.py:140
  77.4 5.8 %collective-permute-start.15 = (bf16[4,16,16,128]{3,2,1,0:T(8,128)(2,1)S(1)}, bf16[4,16,16,128]{3,2,1,0:T(8,128)(2,1)S(1)}, u32[]{:S(2)}, u32[]{:S(2)}) collective-permute-start(bf16[4,16,16,128]{3,2,1,0:T(8,128)(2,1)S(1)} %convert_element_type.262), channel_id=1, source_target_pairs={{8,0},{16,8},{24,16},{32,24},{40,32},{48,40},{56,48},{64,56},{72,6... | collective-permute-start | bytes 786440 | tf_op jit(solution)/shard_map/ppermute | solution.py:28
  83.2 5.3 %collective-permute-start.10 = (bf16[1024,128]{1,0:T(8,128)(2,1)S(1)}, bf16[1024,128]{1,0:T(8,128)(2,1)}, u32[]{:S(2)}, u32[]{:S(2)}) collective-permute-start(bf16[1024,128]{1,0:T(8,128)(2,1)S(1)} %collective-permute-done.9), channel_id=1, source_target_pairs={{0,1},{1,2},{2,3},{3,4},{4,5},{5,6},{6,7},{7,0},{8,9},{9,10},{10,1... | collective-permute-start | bytes 786440 | tf_op jit(solution)/shard_map/ppermute | solution.py:140
  92.8 5.1 %collective-permute-start.11 = (bf16[1024,128]{1,0:T(8,128)(2,1)}, bf16[1024,128]{1,0:T(8,128)(2,1)S(1)}, u32[]{:S(2)}, u32[]{:S(2)}) collective-permute-start(bf16[1024,128]{1,0:T(8,128)(2,1)} %collective-permute-done.10), channel_id=1, source_target_pairs={{0,1},{1,2},{2,3},{3,4},{4,5},{5,6},{6,7},{7,0},{8,9},{9,10},{10,1... | collective-permute-start | bytes 786440 | tf_op jit(solution)/shard_map/ppermute | solution.py:140
  110.4 2.5 %gather_fusion = bf16[8,1024,128]{2,1,0:T(8,128)(2,1)S(1)} fusion(bf16[8,1024,128]{2,1,0:T(8,128)(2,1)} %bitcast_dynamic-update-slice_fusion, s32[1024]{0:T(1024)S(1)} %pad_clamp_fusion), kind=kCustom, calls=%fused_computation | custom fusion | bytes 4194336 | tf_op jit(solution)/shard_map/gather | solution.py:145
  113.5 2.6 %copy.200 = bf16[1024,8,128]{0,2,1:T(8,128)(2,1)} copy(bf16[1024,8,128]{2,0,1:T(8,128)(2,1)S(1)} %bitcast.114) | data formatting | bytes 4194304 | tf_op jit(solution)/shard_map/transpose | solution.py:17
  116.1 2.4 %fusion.206 = f32[64,16,128]{2,1,0:T(8,128)S(1)} fusion(bf16[64,16,1024]{2,1,0:T(8,128)(2,1)} %bitcast.115, bf16[1024,128,1]{1,0,2:T(8,128)(2,1)S(1)} %bitcast.124), kind=kOutput, calls=%fused_computation.314 | convolution fusion | flops 268435456 | bytes 2883584 | tf_op jit(solution)/shard_map/dot_general | solution.py:97
  129.0 8.7 %collective-permute-done.18 = f32[2,2,2,2,17,256]{5,3,4,2,1,0:T(2,128)S(1)} collective-permute-done((f32[2,2,2,2,17,256]{5,3,4,2,1,0:T(2,128)S(1)}, f32[2,2,2,2,17,256]{5,3,4,2,1,0:T(2,128)S(1)}, u32[]{:S(2)}, u32[]{:S(2)}) %collective-permute-start.18) | collective-permute-done | bytes 278560 | tf_op jit(solution)/shard_map/ppermute | solution.py:116
  140.0 8.7 %collective-permute-done.19 = f32[2,2,2,17,256]{4,2,3,1,0:T(2,128)S(1)} collective-permute-done((f32[2,2,2,17,256]{4,2,3,1,0:T(2,128)S(1)}, f32[2,2,2,17,256]{4,2,3,1,0:T(2,128)S(1)}, u32[]{:S(2)}, u32[]{:S(2)}) %collective-permute-start.19) | collective-permute-done | bytes 139296 | tf_op jit(solution)/shard_map/ppermute | solution.py:116
  151.0 8.2 %collective-permute-done.20 = f32[2,2,17,256]{3,1,2,0:T(2,128)S(1)} collective-permute-done((f32[2,2,17,256]{3,1,2,0:T(2,128)S(1)}, f32[2,2,17,256]{3,1,2,0:T(2,128)S(1)}, u32[]{:S(2)}, u32[]{:S(2)}) %collective-permute-start.20) | collective-permute-done | bytes 69664 | tf_op jit(solution)/shard_map/ppermute | solution.py:116
  159.3 2.4 %collective-permute-start.21 = (f32[2,17,256]{2,0,1:T(2,128)S(1)}, f32[2,17,256]{2,0,1:T(2,128)S(1)}, u32[]{:S(2)}, u32[]{:S(2)}) collective-permute-start(f32[2,17,256]{2,0,1:T(2,128)S(1)} %bitcast.135), channel_id=1, source_target_pairs={{0,128},{8,136},{16,144},{24,152},{32,160},{40,168},{48,176},{56,1... | collective-permute-start | bytes 104456 | tf_op jit(solution)/shard_map/ppermute | solution.py:116
  161.7 3.4 %collective-permute-done.21 = f32[2,17,256]{2,0,1:T(2,128)S(1)} collective-permute-done((f32[2,17,256]{2,0,1:T(2,128)S(1)}, f32[2,17,256]{2,0,1:T(2,128)S(1)}, u32[]{:S(2)}, u32[]{:S(2)}) %collective-permute-start.21) | collective-permute-done | bytes 34848 | tf_op jit(solution)/shard_map/ppermute | solution.py:116
  165.2 3.0 %collective-permute-start.22 = (f32[17,256]{1,0:T(8,128)S(1)}, f32[17,256]{1,0:T(8,128)S(1)}, u32[]{:S(2)}, u32[]{:S(2)}) collective-permute-start(f32[17,256]{1,0:T(8,128)S(1)} %bitcast.136), channel_id=1, source_target_pairs={{0,256},{8,264},{16,272},{24,280},{32,288},{40,296},{48,304},{56,3... | collective-permute-start | bytes 52232 | tf_op jit(solution)/shard_map/ppermute | solution.py:116
  168.2 4.2 %collective-permute-done.22 = f32[17,256]{1,0:T(8,128)S(1)} collective-permute-done((f32[17,256]{1,0:T(8,128)S(1)}, f32[17,256]{1,0:T(8,128)S(1)}, u32[]{:S(2)}, u32[]{:S(2)}) %collective-permute-start.22) | collective-permute-done | bytes 17440 | tf_op jit(solution)/shard_map/ppermute | solution.py:116
  (101 shorter events, 58.1 us)
Async XLA Ops:
  1.7 16.1 %collective-permute-start = (bf16[4,16,16,128]{3,2,1,0:T(8,128)(2,1)S(1)}, bf16[4,16,16,128]{3,2,1,0:T(8,128)(2,1)S(1)}, u32[]{:S(2)}, u32[]{:S(2)}) collective-permute-start(bf16[4,16,16,128]{3,2,1,0:T(8,128)(2,1)S(1)} %convert_element_type.234), channel_id=1, source_target_pairs={{8,0},{16,8},{24,16},{32,24},{40,32},{48,40},{56,48},{64,56},{72,6... | collective-permute-start | bytes 786440 | tf_op jit(solution)/shard_map/ppermute | solution.py:28
  12.4 9.8 %collective-permute-start.1 = (bf16[4,16,16,128]{3,2,1,0:T(8,128)(2,1)S(1)}, bf16[4,16,16,128]{3,2,1,0:T(8,128)(2,1)S(1)}, u32[]{:S(2)}, u32[]{:S(2)}) collective-permute-start(bf16[4,16,16,128]{3,2,1,0:T(8,128)(2,1)S(1)} %convert_element_type.234), channel_id=1, source_target_pairs={{0,8},{8,16},{16,24},{24,32},{32,40},{40,48},{48,56},{56,64},{64,7... | collective-permute-start | bytes 786440 | tf_op jit(solution)/shard_map/ppermute | solution.py:27
  15.1 7.2 %copy-start.2 = (f32[4,16,16]{2,1,0:T(8,128)S(1)}, f32[4,16,16]{2,1,0:T(8,128)}, u32[]{:S(2)}) copy-start(f32[4,16,16]{2,1,0:T(8,128)} %param.3) | copy-start | bytes 12292
  22.6 6.5 %collective-permute-start.2 = (bf16[4,16,16,128]{3,2,1,0:T(8,128)(2,1)S(1)}, bf16[4,16,16,128]{3,2,1,0:T(8,128)(2,1)S(1)}, u32[]{:S(2)}, u32[]{:S(2)}) collective-permute-start(bf16[4,16,16,128]{3,2,1,0:T(8,128)(2,1)S(1)} %get-tuple-element.9), channel_id=1, source_target_pairs={{8,0},{16,8},{24,16},{32,24},{40,32},{48,40},{56,48},{64,56},{72,6... | collective-permute-start | bytes 786440 | tf_op jit(solution)/shard_map/ppermute | solution.py:28
  24.6 9.8 %collective-permute-start.3 = (bf16[4,16,16,128]{3,2,1,0:T(8,128)(2,1)S(1)}, bf16[4,16,16,128]{3,2,1,0:T(8,128)(2,1)S(1)}, u32[]{:S(2)}, u32[]{:S(2)}) collective-permute-start(bf16[4,16,16,128]{3,2,1,0:T(8,128)(2,1)S(1)} %get-tuple-element.9), channel_id=1, source_target_pairs={{0,8},{8,16},{16,24},{24,32},{32,40},{40,48},{48,56},{56,64},{64,7... | collective-permute-start | bytes 786440 | tf_op jit(solution)/shard_map/ppermute | solution.py:27
  34.8 6.5 %collective-permute-start.4 = (bf16[4,16,16,128]{3,2,1,0:T(8,128)(2,1)S(1)}, bf16[4,16,16,128]{3,2,1,0:T(8,128)(2,1)S(1)}, u32[]{:S(2)}, u32[]{:S(2)}) collective-permute-start(bf16[4,16,16,128]{3,2,1,0:T(8,128)(2,1)S(1)} %get-tuple-element.7), channel_id=1, source_target_pairs={{8,0},{16,8},{24,16},{32,24},{40,32},{48,40},{56,48},{64,56},{72,6... | collective-permute-start | bytes 786440 | tf_op jit(solution)/shard_map/ppermute | solution.py:28
  36.8 9.8 %collective-permute-start.5 = (bf16[4,16,16,128]{3,2,1,0:T(8,128)(2,1)S(1)}, bf16[4,16,16,128]{3,2,1,0:T(8,128)(2,1)S(1)}, u32[]{:S(2)}, u32[]{:S(2)}) collective-permute-start(bf16[4,16,16,128]{3,2,1,0:T(8,128)(2,1)S(1)} %get-tuple-element.7), channel_id=1, source_target_pairs={{0,8},{8,16},{16,24},{24,32},{32,40},{40,48},{48,56},{56,64},{64,7... | collective-permute-start | bytes 786440 | tf_op jit(solution)/shard_map/ppermute | solution.py:27
  47.0 6.5 %collective-permute-start.6 = (bf16[4,16,16,128]{3,2,1,0:T(8,128)(2,1)S(1)}, bf16[4,16,16,128]{3,2,1,0:T(8,128)(2,1)S(1)}, u32[]{:S(2)}, u32[]{:S(2)}) collective-permute-start(bf16[4,16,16,128]{3,2,1,0:T(8,128)(2,1)S(1)} %get-tuple-element.5), channel_id=1, source_target_pairs={{8,0},{16,8},{24,16},{32,24},{40,32},{48,40},{56,48},{64,56},{72,6... | collective-permute-start | bytes 786440 | tf_op jit(solution)/shard_map/ppermute | solution.py:28
  49.0 9.8 %collective-permute-start.7 = (bf16[4,16,16,128]{3,2,1,0:T(8,128)(2,1)S(1)}, bf16[4,16,16,128]{3,2,1,0:T(8,128)(2,1)S(1)}, u32[]{:S(2)}, u32[]{:S(2)}) collective-permute-start(bf16[4,16,16,128]{3,2,1,0:T(8,128)(2,1)S(1)} %get-tuple-element.5), channel_id=1, source_target_pairs={{0,8},{8,16},{16,24},{24,32},{32,40},{40,48},{48,56},{56,64},{64,7... | collective-permute-start | bytes 786440 | tf_op jit(solution)/shard_map/ppermute | solution.py:27
  59.3 8.6 %collective-permute-start.8 = (bf16[1024,128]{1,0:T(8,128)(2,1)S(1)}, bf16[1024,128]{1,0:T(8,128)(2,1)S(1)}, u32[]{:S(2)}, u32[]{:S(2)}) collective-permute-start(bf16[1024,128]{1,0:T(8,128)(2,1)S(1)} %bitcast.121), channel_id=1, source_target_pairs={{0,1},{1,2},{2,3},{3,4},{4,5},{5,6},{6,7},{7,0},{8,9},{9,10},{10,1... | collective-permute-start | bytes 786440 | tf_op jit(solution)/shard_map/ppermute | solution.py:140
  67.9 15.3 %collective-permute-start.9 = (bf16[1024,128]{1,0:T(8,128)(2,1)S(1)}, bf16[1024,128]{1,0:T(8,128)(2,1)S(1)}, u32[]{:S(2)}, u32[]{:S(2)}) collective-permute-start(bf16[1024,128]{1,0:T(8,128)(2,1)S(1)} %collective-permute-done.8), channel_id=1, source_target_pairs={{0,1},{1,2},{2,3},{3,4},{4,5},{5,6},{6,7},{7,0},{8,9},{9,10},{10,1... | collective-permute-start | bytes 786440 | tf_op jit(solution)/shard_map/ppermute | solution.py:140
  73.6 17.2 %collective-permute-start.12 = (bf16[1024,128]{1,0:T(8,128)(2,1)S(1)}, bf16[1024,128]{1,0:T(8,128)(2,1)S(1)}, u32[]{:S(2)}, u32[]{:S(2)}) collective-permute-start(bf16[1024,128]{1,0:T(8,128)(2,1)S(1)} %bitcast.122), channel_id=1, source_target_pairs={{1,0},{2,1},{3,2},{4,3},{5,4},{6,5},{7,6},{0,7},{9,8},{10,9},{11,1... | collective-permute-start | bytes 786440 | tf_op jit(solution)/shard_map/ppermute | solution.py:142
  75.5 17.2 %collective-permute-start.16 = (bf16[4,16,16,128]{3,2,1,0:T(8,128)(2,1)S(1)}, bf16[4,16,16,128]{3,2,1,0:T(8,128)(2,1)S(1)}, u32[]{:S(2)}, u32[]{:S(2)}) collective-permute-start(bf16[4,16,16,128]{3,2,1,0:T(8,128)(2,1)S(1)} %convert_element_type.262), channel_id=1, source_target_pairs={{0,8},{8,16},{16,24},{24,32},{32,40},{40,48},{48,56},{56,64},{64,7... | collective-permute-start | bytes 786440 | tf_op jit(solution)/shard_map/ppermute | solution.py:27
  77.4 15.3 %collective-permute-start.15 = (bf16[4,16,16,128]{3,2,1,0:T(8,128)(2,1)S(1)}, bf16[4,16,16,128]{3,2,1,0:T(8,128)(2,1)S(1)}, u32[]{:S(2)}, u32[]{:S(2)}) collective-permute-start(bf16[4,16,16,128]{3,2,1,0:T(8,128)(2,1)S(1)} %convert_element_type.262), channel_id=1, source_target_pairs={{8,0},{16,8},{24,16},{32,24},{40,32},{48,40},{56,48},{64,56},{72,6... | collective-permute-start | bytes 786440 | tf_op jit(solution)/shard_map/ppermute | solution.py:28
  83.2 9.6 %collective-permute-start.10 = (bf16[1024,128]{1,0:T(8,128)(2,1)S(1)}, bf16[1024,128]{1,0:T(8,128)(2,1)}, u32[]{:S(2)}, u32[]{:S(2)}) collective-permute-start(bf16[1024,128]{1,0:T(8,128)(2,1)S(1)} %collective-permute-done.9), channel_id=1, source_target_pairs={{0,1},{1,2},{2,3},{3,4},{4,5},{5,6},{6,7},{7,0},{8,9},{9,10},{10,1... | collective-permute-start | bytes 786440 | tf_op jit(solution)/shard_map/ppermute | solution.py:140
  90.7 9.5 %collective-permute-start.13 = (bf16[1024,128]{1,0:T(8,128)(2,1)S(1)}, bf16[1024,128]{1,0:T(8,128)(2,1)S(1)}, u32[]{:S(2)}, u32[]{:S(2)}) collective-permute-start(bf16[1024,128]{1,0:T(8,128)(2,1)S(1)} %collective-permute-done.12), channel_id=1, source_target_pairs={{1,0},{2,1},{3,2},{4,3},{5,4},{6,5},{7,6},{0,7},{9,8},{10,9},{11,1... | collective-permute-start | bytes 786440 | tf_op jit(solution)/shard_map/ppermute | solution.py:142
  92.8 9.3 %collective-permute-start.11 = (bf16[1024,128]{1,0:T(8,128)(2,1)}, bf16[1024,128]{1,0:T(8,128)(2,1)S(1)}, u32[]{:S(2)}, u32[]{:S(2)}) collective-permute-start(bf16[1024,128]{1,0:T(8,128)(2,1)} %collective-permute-done.10), channel_id=1, source_target_pairs={{0,1},{1,2},{2,3},{3,4},{4,5},{5,6},{6,7},{7,0},{8,9},{9,10},{10,1... | collective-permute-start | bytes 786440 | tf_op jit(solution)/shard_map/ppermute | solution.py:140
  100.2 9.5 %collective-permute-start.14 = (bf16[1024,128]{1,0:T(8,128)(2,1)S(1)}, bf16[1024,128]{1,0:T(8,128)(2,1)S(1)}, u32[]{:S(2)}, u32[]{:S(2)}) collective-permute-start(bf16[1024,128]{1,0:T(8,128)(2,1)S(1)} %collective-permute-done.13), channel_id=1, source_target_pairs={{1,0},{2,1},{3,2},{4,3},{5,4},{6,5},{7,6},{0,7},{9,8},{10,9},{11,1... | collective-permute-start | bytes 786440 | tf_op jit(solution)/shard_map/ppermute | solution.py:142
  122.3 4.0 %collective-permute-start.17 = (f32[2,2,2,2,2,17,256]{6,4,5,3,2,1,0:T(2,128)}, f32[2,2,2,2,2,17,256]{6,4,5,3,2,1,0:T(2,128)S(1)}, u32[]{:S(2)}, u32[]{:S(2)}) collective-permute-start(f32[2,2,2,2,2,17,256]{6,4,5,3,2,1,0:T(2,128)} %copy.205), channel_id=1, source_target_pairs={{0,8},{8,0},{16,24},{24,16},{32,40},{40,32},{48,56},{56,48},{64,72... | collective-permute-start | bytes 1671176 | tf_op jit(solution)/shard_map/ppermute | solution.py:116
  127.0 10.6 %collective-permute-start.18 = (f32[2,2,2,2,17,256]{5,3,4,2,1,0:T(2,128)S(1)}, f32[2,2,2,2,17,256]{5,3,4,2,1,0:T(2,128)S(1)}, u32[]{:S(2)}, u32[]{:S(2)}) collective-permute-start(f32[2,2,2,2,17,256]{5,3,4,2,1,0:T(2,128)S(1)} %select_bitcast_fusion.1), channel_id=1, source_target_pairs={{0,16},{8,24},{16,0},{24,8},{32,48},{40,56},{48,32},{56,40},{64,80... | collective-permute-start | bytes 835592 | tf_op jit(solution)/shard_map/ppermute | solution.py:116
  138.1 10.7 %collective-permute-start.19 = (f32[2,2,2,17,256]{4,2,3,1,0:T(2,128)S(1)}, f32[2,2,2,17,256]{4,2,3,1,0:T(2,128)S(1)}, u32[]{:S(2)}, u32[]{:S(2)}) collective-permute-start(f32[2,2,2,17,256]{4,2,3,1,0:T(2,128)S(1)} %bitcast.133), channel_id=1, source_target_pairs={{0,32},{8,40},{16,48},{24,56},{32,0},{40,8},{48,16},{56,24},{64,96... | collective-permute-start | bytes 417800 | tf_op jit(solution)/shard_map/ppermute | solution.py:116
  149.0 10.1 %collective-permute-start.20 = (f32[2,2,17,256]{3,1,2,0:T(2,128)S(1)}, f32[2,2,17,256]{3,1,2,0:T(2,128)S(1)}, u32[]{:S(2)}, u32[]{:S(2)}) collective-permute-start(f32[2,2,17,256]{3,1,2,0:T(2,128)S(1)} %bitcast.134), channel_id=1, source_target_pairs={{0,64},{8,72},{16,80},{24,88},{32,96},{40,104},{48,112},{56,120},{... | collective-permute-start | bytes 208904 | tf_op jit(solution)/shard_map/ppermute | solution.py:116
  159.3 5.8 %collective-permute-start.21 = (f32[2,17,256]{2,0,1:T(2,128)S(1)}, f32[2,17,256]{2,0,1:T(2,128)S(1)}, u32[]{:S(2)}, u32[]{:S(2)}) collective-permute-start(f32[2,17,256]{2,0,1:T(2,128)S(1)} %bitcast.135), channel_id=1, source_target_pairs={{0,128},{8,136},{16,144},{24,152},{32,160},{40,168},{48,176},{56,1... | collective-permute-start | bytes 104456 | tf_op jit(solution)/shard_map/ppermute | solution.py:116
  165.2 7.2 %collective-permute-start.22 = (f32[17,256]{1,0:T(8,128)S(1)}, f32[17,256]{1,0:T(8,128)S(1)}, u32[]{:S(2)}, u32[]{:S(2)}) collective-permute-start(f32[17,256]{1,0:T(8,128)S(1)} %bitcast.136), channel_id=1, source_target_pairs={{0,256},{8,264},{16,272},{24,280},{32,288},{40,296},{48,304},{56,3... | collective-permute-start | bytes 52232 | tf_op jit(solution)/shard_map/ppermute | solution.py:116
  (2 other events, 9.6 us)
